TPU v7x, 256 devices: a whole 4x4x8 slice. The times are simulated.
256 devices in a mesh: dp: 32 (over x_lo, z, core), blk: 8 (over y, x_hi).
Axes of the slice: x: 4 (x_hi: 2, x_lo: 2; x = x_hi * 2 + x_lo), y: 4, z: 8, core: 2. Of those that a mesh axis runs over, the one named last changes fastest.
Arguments:
- inputs: bfloat16 [8, 16384, 4096], P('blk', 'dp'), may hold values from -6 to 6
- out_grads: bfloat16 [8, 16384, 4096], P('blk', 'dp'), may hold values from -8 to 8
- test_matrix: bfloat16 [8, 4096, 256], P('blk'), may hold values from -6 to 6
- momentum: bfloat16 [8, 4096, 4096], P(None, 'blk', 'dp'), may hold values from -6 to 6
Outputs:
- update: bfloat16 [8, 4096, 4096], P(None, 'blk', 'dp')
All inputs are finite; a program needn't handle non-finite values.
Results may differ from a plain program's by a relative error of at most 0.0035.
Values may be sent and summed in bfloat16 or wider, within the bound.
No kernel may reach another device: no remote copies, remote signals or barrier semaphores. Data moves between devices by JAX's collectives and lax.ppermute only.
A program may use at most 128 MiB of HBM per device.

v0:
```python
import functools
import jax
import jax.numpy as jnp
from jax import lax
from jax.sharding import Mesh
from jax.sharding import PartitionSpec as P
from jax.experimental import pallas as pl
from jax.experimental.pallas import tpu as pltpu

DP = ("dp_0", "dp_1", "dp_2")


def filled_up(lines, devices):
    spare = -len(lines) % devices
    return jnp.pad(lines, [(0, spare)] + [(0, 0)] * (lines.ndim - 1))


def copy_for_each(x, axis):
    devices = lax.axis_size(axis)
    return lax.all_to_all(jnp.broadcast_to(x[None], (devices, *x.shape)), axis, 0, 0, tiled=True)


def in_order(blocks, dim):
    blocks = jnp.moveaxis(blocks, 0, dim)
    lengths = blocks.shape
    return blocks.reshape(*lengths[:dim], lengths[dim] * lengths[dim + 1], *lengths[dim + 2 :])


def whole_of(x, axes, dim):
    far, near = axes
    first = copy_for_each(x, far)
    blocks = jnp.swapaxes(copy_for_each(first, near), 0, 1)
    return in_order(blocks.reshape(-1, *x.shape), dim)


def in_blocks(x, dim, devices):
    lengths = x.shape
    blocks = x.reshape(*lengths[:dim], devices, lengths[dim] // devices, *lengths[dim + 1 :])
    return jnp.moveaxis(blocks, dim, 0)


def sum_at_owner(x, axis, dim):
    blocks = in_blocks(x, dim, lax.axis_size(axis))
    arrived = lax.all_to_all(blocks, axis, split_axis=0, concat_axis=0, tiled=True)
    return arrived.sum(axis=0)


def sum_by_axis(x, axes, dim):
    far, near = axes
    blocks = in_blocks(x, dim, lax.axis_size(far))
    nearer = sum_at_owner(blocks, near, dim + 1).astype(jnp.bfloat16)
    arrived = lax.all_to_all(nearer, far, split_axis=0, concat_axis=0, tiled=True)
    return arrived.astype(jnp.float32).sum(axis=0)


def total_of(x, axes):
    lines = x.reshape(-1, x.shape[-1])
    padded = filled_up(lines, lax.axis_size(axes[0]) * lax.axis_size(axes[1]))
    whole = whole_of(sum_by_axis(padded, axes, 0).astype(jnp.bfloat16), axes, 0)
    return lax.slice_in_dim(whole, 0, len(lines)).reshape(x.shape)


def collect(x, axis, dim):
    blocks = copy_for_each(x, axis)
    return in_order(blocks, dim)


def total_of_2(x, axes):
    lines = x.reshape(-1, x.shape[-1])
    own = sum_at_owner(filled_up(lines, lax.axis_size(axes)), axes, 0)
    whole = collect(own, axes, 0)
    return whole[: len(lines)].reshape(x.shape)


def butterfly_sum(x, axes, masks):
    size = 1
    for a in axes:
        size *= lax.axis_size(a)
    for m in masks:
        x = x + lax.ppermute(x, axes, [(i, i ^ m) for i in range(size)])
    return x


def shifted(x, axis, s):
    n = lax.axis_size(axis)
    return lax.ppermute(x, axis, [(j, (j + s) % n) for j in range(n)])


def spread(stack, axis):
    n = lax.axis_size(axis)
    me = lax.axis_index(axis)
    mine = jnp.roll(stack, -me, axis=0)
    pieces = [mine[0]] + [shifted(mine[s], axis, s) for s in range(1, n)]
    ordered = jnp.stack([pieces[(-i) % n] for i in range(n)])
    return jnp.roll(ordered, me, axis=0)


def gather_all(x, axis):
    n = lax.axis_size(axis)
    me = lax.axis_index(axis)
    pieces = [x] + [shifted(x, axis, s) for s in range(1, n)]
    ordered = jnp.stack([pieces[(-i) % n] for i in range(n)])
    return jnp.roll(ordered, me, axis=0)


def ring_sum(x, axis):
    n = lax.axis_size(axis)
    parts = x.reshape(n, x.shape[0] // n, *x.shape[1:])
    own = lax.all_to_all(parts, axis, 0, 0, tiled=True).sum(axis=0)
    return collect(own, axis, 0)


def inner_gram(columns):
    return lax.dot_general(
        columns, columns, (((0,), (0,)), ((), ())), precision=lax.Precision.HIGHEST
    )


def mm(a, b):
    return jnp.dot(a, b, precision=lax.Precision.HIGHEST)


def _factor_kernel(a_ref, w_ref, r_ref, panel_rows):
    n = a_ref.shape[0]
    rows_i = lax.broadcasted_iota(jnp.int32, (n, n), 0)
    cols_i = lax.broadcasted_iota(jnp.int32, (n, n), 1)
    r_ref[:, :n] = a_ref[...]
    r_ref[:, n:] = jnp.where(rows_i == cols_i, 1.0, 0.0).astype(jnp.float32)
    sub = lax.broadcasted_iota(jnp.int32, (panel_rows, 1), 0)
    lane = lax.broadcasted_iota(jnp.int32, (panel_rows, 128), 1)
    lane_wide = lax.broadcasted_iota(jnp.int32, (1, 2 * n), 1)
    for p in range(n // panel_rows):
        r0 = panel_rows * p
        panel = r_ref[r0:r0 + panel_rows, :]
        for r in range(panel_rows):
            j = r0 + r
            part = panel[:, (j // 128) * 128:(j // 128 + 1) * 128]
            column = jnp.sum(jnp.where(lane == (j % 128), part, 0.0), axis=1, keepdims=True)
            inv = lax.rsqrt(column[r:r + 1, :])
            row = jnp.where(lane_wide < j, 0.0, panel[r:r + 1, :] * inv)
            mult = jnp.where(sub > r, column * inv, 0.0)
            panel = jnp.where(sub == r, row, panel - mult * row)
        r_ref[r0:r0 + panel_rows, :] = panel
        low = r0 + panel_rows
        if low < n:
            outer = lax.dot_general(
                panel[:, :n], panel, (((0,), (0,)), ((), ())),
                precision=lax.Precision.HIGHEST, preferred_element_type=jnp.float32,
            )
            r_ref[low:, :] = r_ref[low:, :] - outer[low:, :]
    w_ref[...] = r_ref[:, n:]


def inverse_factor(matrix):
    n = matrix.shape[0]
    sym = (matrix + matrix.T) * 0.5
    return pl.pallas_call(
        functools.partial(_factor_kernel, panel_rows=64),
        out_shape=jax.ShapeDtypeStruct((n, n), jnp.float32),
        scratch_shapes=[pltpu.VMEM((n, 2 * n), jnp.float32)],
    )(sym)


def cholesky_pass(columns, gram_matrix):
    return mm(columns, inverse_factor(gram_matrix).T)


def shards(inputs, out_grads, test_matrix, momentum):
    features = inputs[0]
    errors = out_grads[0]
    probes = test_matrix[0]
    replicas = lax.axis_size(DP)
    scale = 1.0 / (features.shape[1] * features.shape[0] * replicas)
    projected = jnp.dot(features, probes, preferred_element_type=jnp.float32).astype(jnp.bfloat16)
    token_gram = lax.dot_general(
        errors, errors, (((1,), (1,)), ((), ())), preferred_element_type=jnp.float32
    ).astype(jnp.bfloat16)
    mixed_rows = jnp.dot(token_gram, projected, preferred_element_type=jnp.float32).astype(
        jnp.bfloat16
    )
    sketch_term = (
        lax.dot_general(
            features, mixed_rows, (((0,), (0,)), ((), ())), preferred_element_type=jnp.float32
        )
        * scale
    )
    sketch = total_of(sketch_term, (("dp_0", "dp_1"), "dp_2")).astype(jnp.float32)
    basis = cholesky_pass(sketch, inner_gram(sketch)).astype(jnp.bfloat16)
    reduced = jnp.dot(features, basis, preferred_element_type=jnp.float32).astype(jnp.bfloat16)
    shaped = jnp.dot(token_gram, reduced, preferred_element_type=jnp.float32).astype(jnp.bfloat16)
    core_term = (
        lax.dot_general(
            reduced, shaped, (((0,), (0,)), ((), ())), preferred_element_type=jnp.float32
        )
        * scale
    )
    core_matrix = ring_sum(butterfly_sum(core_term, DP, (1, 16)), "dp_1")
    shifted = core_matrix + jnp.eye(core_matrix.shape[0], dtype=jnp.float32)
    inverse = inverse_factor(shifted)
    factor = mm(inverse.T, mm(inverse, core_matrix))
    blocks = spread(momentum, "blk")
    columns = blocks.reshape(-1, blocks.shape[-1])
    coeffs = lax.dot_general(
        basis, columns, (((0,), (0,)), ((), ())), preferred_element_type=jnp.float32
    )
    scaled = jnp.dot(factor, coeffs, precision=lax.Precision.HIGHEST).astype(jnp.bfloat16)
    fresh = (
        columns.astype(jnp.float32) - jnp.dot(basis, scaled, preferred_element_type=jnp.float32)
    ).astype(jnp.bfloat16)
    return spread(fresh.reshape(blocks.shape), "blk")


def solution(mesh):
    torus = Mesh(mesh.devices.reshape(2, 8, 2, mesh.shape["blk"]), ("dp_0", "dp_1", "dp_2", "blk"))
    in_specs = (P("blk", DP, None), P("blk", DP, None), P("blk", None, None), P(None, "blk", DP))
    out_specs = P(None, "blk", DP)
    return jax.shard_map(
        shards, mesh=torus, in_specs=in_specs, out_specs=out_specs, check_vma=False
    )
```

profile of v0, /device:TPU:8, one launch (start us, length us, event | category | flops | bytes accessed | tf_op | source)
XLA Modules:
  0.0 265.1 jit_solution(9402345454683955309)
XLA Ops:
  0.0 6.0 %fusion.13 = bf16[512,512]{1,0:T(8,128)(2,1)S(1)} fusion(bf16[1,512,4096]{2,1,0:T(8,128)(2,1)} %param.7), kind=kOutput, calls=%fused_computation.25 | convolution fusion | flops 2147745792 | bytes 4718592 | tf_op jit(solution)/shard_map/dot_general | solution.py:175
  7.3 5.9 %fusion = f32[4096,256]{0,1:T(8,128)} fusion(bf16[1,512,4096]{2,1,0:T(8,128)(2,1)} %param.6, bf16[512,512]{1,0:T(8,128)(2,1)S(1)} %fusion.13, bf16[512,256]{1,0:T(8,128)(2,1)S(1)} %fusion.16), kind=kOutput, calls=%fused_computation.1 | convolution fusion | flops 1209139200 | bytes 9175040 | tf_op jit(solution)/shard_map/dot_general | solution.py:182
  13.2 6.6 %reshape_reshape.6 = f32[16,2,128,256]{2,1,0,3:T(2,128)} reshape(f32[4096,256]{0,1:T(8,128)} %fusion) | data formatting | bytes 8388608 | tf_op jit(solution)/shard_map/reshape;reshape | solution.py:38
  19.8 2.5 copy.44
  22.3 8.2 %all_to_all.30 = f32[2,16,128,256]{2,1,3,0:T(8,128)} all-to-all(f32[2,16,128,256]{2,1,3,0:T(8,128)S(1)} %bitcast.129), channel_id=1, replica_groups=mesh['dp_0'=2,'dp_1'=8,'dp_2'=2,'blk'=8] {'dp_2'}, dimensions={0} | all-to-all | bytes 8388608 | tf_op jit(solution)/shard_map/all_to_all | solution.py:44
  30.5 2.6 reduce_sum.30
  33.4 36.3 %all_to_all.31 = bf16[16,128,256]{1,2,0:T(8,128)(2,1)S(1)} all-to-all(bf16[16,128,256]{1,2,0:T(8,128)(2,1)S(1)} %copy.21), channel_id=1, replica_groups=mesh['dp_0'=2,'dp_1'=8,'dp_2'=2,'blk'=8] {'dp_0','dp_1'}, dimensions={0} | all-to-all | bytes 2097152 | tf_op jit(solution)/shard_map/all_to_all | solution.py:52
  71.0 4.8 %all-to-all-start.2 = ((bf16[16,128,256]{2,1,0:T(8,128)(2,1)}), bf16[16,128,256]{2,1,0:T(8,128)(2,1)S(1)}, u32[]{:S(2)}, u32[]{:S(2)}) async-start(bf16[16,128,256]{2,1,0:T(8,128)(2,1)} %broadcast_in_dim.6), calls=%async_computation.2 | async-start | bytes 2097152 | tf_op jit(solution)/shard_map/all_to_all | solution.py:20
  75.8 1.6 fusion.34
  78.3 2.6 collective-permute-start
  80.9 3.1 %collective-permute-start.1 = (bf16[512,128]{1,0:T(8,128)(2,1)}, bf16[512,128]{1,0:T(8,128)(2,1)}, u32[]{:S(2)}, u32[]{:S(2)}) collective-permute-start(bf16[512,128]{1,0:T(8,128)(2,1)} %get-tuple-element.19), channel_id=1, source_target_pairs={{0,6},{1,7},{2,0},{3,1},{4,2},{5,3},{6,4},{7,5},{8,14},{9,15},{10,... | collective-permute-start | bytes 393224 | tf_op jit(solution)/shard_map/ppermute | solution.py:86
  85.3 3.7 %collective-permute-start.4 = (bf16[512,128]{1,0:T(8,128)(2,1)S(1)}, bf16[512,128]{1,0:T(8,128)(2,1)}, u32[]{:S(2)}, u32[]{:S(2)}) collective-permute-start(bf16[512,128]{1,0:T(8,128)(2,1)S(1)} %get-tuple-element.16), channel_id=1, source_target_pairs={{0,3},{1,4},{2,5},{3,6},{4,7},{5,0},{6,1},{7,2},{8,11},{9,12},{10,... | collective-permute-start | bytes 393224 | tf_op jit(solution)/shard_map/ppermute | solution.py:86
  89.0 14.0 %all-to-all-done.2 = bf16[16,128,256]{2,1,0:T(8,128)(2,1)S(1)} async-done(((bf16[16,128,256]{2,1,0:T(8,128)(2,1)}), bf16[16,128,256]{2,1,0:T(8,128)(2,1)S(1)}, u32[]{:S(2)}, u32[]{:S(2)}) %all-to-all-start.2) | async-done | bytes 1048608 | tf_op jit(solution)/shard_map/all_to_all | solution.py:20
  103.2 5.7 %all_to_all.32 = bf16[2,16,128,256]{3,2,1,0:T(8,128)(2,1)S(1)} all-to-all(bf16[2,16,128,256]{3,2,1,0:T(8,128)(2,1)S(1)} %broadcast_in_dim.7), channel_id=1, replica_groups=mesh['dp_0'=2,'dp_1'=8,'dp_2'=2,'blk'=8] {'dp_2'}, dimensions={0} | all-to-all | bytes 4194304 | tf_op jit(solution)/shard_map/all_to_all | solution.py:20
  108.8 1.3 copy-done.3
  111.8 26.8 %shard_map.46 = f32[256,256]{1,0:T(8,128)} custom-call(f32[256,256]{1,0:T(8,128)} %fusion.36.a_ref), custom_call_target="tpu_custom_call" | custom-call | tf_op jit(solution)/shard_map/pallas_call | solution.py:157
  138.7 1.8 copy.24
  140.5 1.8 convolution_convert_fusion
  142.3 1.3 copy-done.1
  143.6 1.3 fusion.21
  145.8 1.6 bitcast_dynamic-update-slice_fusion.13
  147.3 11.4 %collective-permute-start.5 = (bf16[512,128]{1,0:T(8,128)(2,1)S(1)}, bf16[512,128]{1,0:T(8,128)(2,1)S(1)}, u32[]{:S(2)}, u32[]{:S(2)}) collective-permute-start(bf16[512,128]{1,0:T(8,128)(2,1)S(1)} %get-tuple-element.15), channel_id=1, source_target_pairs={{0,2},{1,3},{2,4},{3,5},{4,6},{5,7},{6,0},{7,1},{8,10},{9,11},{10,... | collective-permute-start | bytes 393224 | tf_op jit(solution)/shard_map/ppermute | solution.py:86
  158.8 1.6 bitcast_dynamic-update-slice_fusion.12
  160.3 2.7 %collective-permute-start.6 = (bf16[512,128]{1,0:T(8,128)(2,1)S(1)}, bf16[512,128]{1,0:T(8,128)(2,1)S(1)}, u32[]{:S(2)}, u32[]{:S(2)}) collective-permute-start(bf16[512,128]{1,0:T(8,128)(2,1)S(1)} %get-tuple-element.14), channel_id=1, source_target_pairs={{0,1},{1,2},{2,3},{3,4},{4,5},{5,6},{6,7},{7,0},{8,9},{9,10},{10,1... | collective-permute-start | bytes 393224 | tf_op jit(solution)/shard_map/ppermute | solution.py:86
  163.2 1.6 bitcast_dynamic-update-slice_fusion.11
  164.8 1.6 bitcast_dynamic-update-slice_fusion.10
  166.4 5.8 %collective-permute-done.8 = f32[256,256]{1,0:T(8,128)S(1)} collective-permute-done((f32[256,256]{1,0:T(8,128)S(1)}, f32[256,256]{1,0:T(8,128)S(1)}, u32[]{:S(2)}, u32[]{:S(2)}) %collective-permute-start.8) | collective-permute-done | bytes 262176 | tf_op jit(solution)/shard_map/ppermute | solution.py:80
  172.9 4.3 %all-to-all-start.4 = ((f32[8,32,256]{2,1,0:T(8,128)}), f32[8,32,256]{2,1,0:T(8,128)S(1)}, u32[]{:S(2)}, u32[]{:S(2)}) async-start(f32[8,32,256]{2,1,0:T(8,128)} %bitcast.27), calls=%async_computation.4 | async-start | bytes 524288 | tf_op jit(solution)/shard_map/all_to_all | solution.py:109
  177.2 1.6 bitcast_dynamic-update-slice_fusion.9
  179.4 9.0 %all-to-all-done.4 = f32[8,32,256]{2,1,0:T(8,128)S(1)} async-done(((f32[8,32,256]{2,1,0:T(8,128)}), f32[8,32,256]{2,1,0:T(8,128)S(1)}, u32[]{:S(2)}, u32[]{:S(2)}) %all-to-all-start.4) | async-done | bytes 262176 | tf_op jit(solution)/shard_map/all_to_all | solution.py:109
  189.2 3.4 %all-to-all-start.5 = ((f32[8,32,256]{2,1,0:T(8,128)}), f32[8,32,256]{2,1,0:T(8,128)S(1)}, u32[]{:S(2)}, u32[]{:S(2)}) async-start(f32[8,32,256]{2,1,0:T(8,128)} %broadcast_in_dim.8), calls=%async_computation.5 | async-start | bytes 524288 | tf_op jit(solution)/shard_map/all_to_all | solution.py:20
  193.3 1.6 fusion.33
  195.7 7.3 %all-to-all-done.5 = f32[8,32,256]{2,1,0:T(8,128)S(1)} async-done(((f32[8,32,256]{2,1,0:T(8,128)}), f32[8,32,256]{2,1,0:T(8,128)S(1)}, u32[]{:S(2)}, u32[]{:S(2)}) %all-to-all-start.5) | async-done | bytes 262176 | tf_op jit(solution)/shard_map/all_to_all | solution.py:20
  203.9 1.7 convert_add_fusion
  205.5 1.8 copy.28
  207.3 1.8 fusion.35.a_ref
  209.1 26.8 %shard_map.47 = f32[256,256]{1,0:T(8,128)} custom-call(f32[256,256]{1,0:T(8,128)} %fusion.35.a_ref), custom_call_target="tpu_custom_call" | custom-call | tf_op jit(solution)/shard_map/pallas_call | solution.py:157
  235.9 1.3 fusion.38
  237.3 1.5 fusion.39
  239.2 2.3 fusion.1
  242.0 3.0 %collective-permute-start.9 = (bf16[512,128]{1,0:T(8,128)(2,1)S(1)}, bf16[512,128]{1,0:T(8,128)(2,1)S(1)}, u32[]{:S(2)}, u32[]{:S(2)}) collective-permute-start(bf16[512,128]{1,0:T(8,128)(2,1)S(1)} %get-tuple-element.12), channel_id=1, source_target_pairs={{0,7},{1,0},{2,1},{3,2},{4,3},{5,4},{6,5},{7,6},{8,15},{9,8},{10,9... | collective-permute-start | bytes 393224 | tf_op jit(solution)/shard_map/ppermute | solution.py:86
  245.0 1.7 collective-permute-start.10
  246.6 1.4 collective-permute-start.11
  249.2 3.7 %collective-permute-start.13 = (bf16[512,128]{1,0:T(8,128)(2,1)S(1)}, bf16[512,128]{1,0:T(8,128)(2,1)S(1)}, u32[]{:S(2)}, u32[]{:S(2)}) collective-permute-start(bf16[512,128]{1,0:T(8,128)(2,1)S(1)} %get-tuple-element.8), channel_id=1, source_target_pairs={{0,3},{1,4},{2,5},{3,6},{4,7},{5,0},{6,1},{7,2},{8,11},{9,12},{10,... | collective-permute-start | bytes 393224 | tf_op jit(solution)/shard_map/ppermute | solution.py:86
  253.9 2.2 collective-permute-done.10
  256.2 1.9 collective-permute-done.13
  259.3 4.1 %collective-permute-done.15 = bf16[512,128]{1,0:T(8,128)(2,1)S(1)} collective-permute-done((bf16[512,128]{1,0:T(8,128)(2,1)S(1)}, bf16[512,128]{1,0:T(8,128)(2,1)S(1)}, u32[]{:S(2)}, u32[]{:S(2)}) %collective-permute-start.15) | collective-permute-done | bytes 131104 | tf_op jit(solution)/shard_map/ppermute | solution.py:86
  263.5 1.4 fusion.31
  (64 shorter events, 16.7 us)
Async XLA Ops:
  0.0 6.0 %copy-start = (bf16[1,4096,256]{2,1,0:T(8,128)(2,1)S(1)}, bf16[1,4096,256]{2,1,0:T(8,128)(2,1)}, u32[]{:S(2)}) copy-start(bf16[1,4096,256]{2,1,0:T(8,128)(2,1)} %param.8) | copy-start | bytes 6291460
  0.0 6.0 %copy-start.4 = (bf16[1,512,4096]{2,1,0:T(8,128)(2,1)S(1)}, bf16[1,512,4096]{2,1,0:T(8,128)(2,1)}, u32[]{:S(2)}) copy-start(bf16[1,512,4096]{2,1,0:T(8,128)(2,1)} %param.6) | copy-start | bytes 12582916
  6.0 1.3 copy-start.6
  71.0 31.9 %all-to-all-start.2 = ((bf16[16,128,256]{2,1,0:T(8,128)(2,1)}), bf16[16,128,256]{2,1,0:T(8,128)(2,1)S(1)}, u32[]{:S(2)}, u32[]{:S(2)}) async-start(bf16[16,128,256]{2,1,0:T(8,128)(2,1)} %broadcast_in_dim.6), calls=%async_computation.2 | async-start | bytes 2097152 | tf_op jit(solution)/shard_map/all_to_all | solution.py:20
  78.3 67.3 %collective-permute-start = (bf16[512,128]{1,0:T(8,128)(2,1)}, bf16[512,128]{1,0:T(8,128)(2,1)}, u32[]{:S(2)}, u32[]{:S(2)}) collective-permute-start(bf16[512,128]{1,0:T(8,128)(2,1)} %get-tuple-element.20), channel_id=1, source_target_pairs={{0,7},{1,0},{2,1},{3,2},{4,3},{5,4},{6,5},{7,6},{8,15},{9,8},{10,9... | collective-permute-start | bytes 393224 | tf_op jit(solution)/shard_map/ppermute | solution.py:86
  80.9 66.4 %collective-permute-start.1 = (bf16[512,128]{1,0:T(8,128)(2,1)}, bf16[512,128]{1,0:T(8,128)(2,1)}, u32[]{:S(2)}, u32[]{:S(2)}) collective-permute-start(bf16[512,128]{1,0:T(8,128)(2,1)} %get-tuple-element.19), channel_id=1, source_target_pairs={{0,6},{1,7},{2,0},{3,1},{4,2},{5,3},{6,4},{7,5},{8,14},{9,15},{10,... | collective-permute-start | bytes 393224 | tf_op jit(solution)/shard_map/ppermute | solution.py:86
  84.0 79.1 %collective-permute-start.2 = (bf16[512,128]{1,0:T(8,128)(2,1)}, bf16[512,128]{1,0:T(8,128)(2,1)}, u32[]{:S(2)}, u32[]{:S(2)}) collective-permute-start(bf16[512,128]{1,0:T(8,128)(2,1)} %get-tuple-element.18), channel_id=1, source_target_pairs={{0,5},{1,6},{2,7},{3,0},{4,1},{5,2},{6,3},{7,4},{8,13},{9,14},{10,... | collective-permute-start | bytes 393224 | tf_op jit(solution)/shard_map/ppermute | solution.py:86
  84.3 80.5 %collective-permute-start.3 = (bf16[512,128]{1,0:T(8,128)(2,1)}, bf16[512,128]{1,0:T(8,128)(2,1)}, u32[]{:S(2)}, u32[]{:S(2)}) collective-permute-start(bf16[512,128]{1,0:T(8,128)(2,1)} %get-tuple-element.17), channel_id=1, source_target_pairs={{0,4},{1,5},{2,6},{3,7},{4,0},{5,1},{6,2},{7,3},{8,12},{9,13},{10,... | collective-permute-start | bytes 393224 | tf_op jit(solution)/shard_map/ppermute | solution.py:86
  85.3 91.9 %collective-permute-start.4 = (bf16[512,128]{1,0:T(8,128)(2,1)S(1)}, bf16[512,128]{1,0:T(8,128)(2,1)}, u32[]{:S(2)}, u32[]{:S(2)}) collective-permute-start(bf16[512,128]{1,0:T(8,128)(2,1)S(1)} %get-tuple-element.16), channel_id=1, source_target_pairs={{0,3},{1,4},{2,5},{3,6},{4,7},{5,0},{6,1},{7,2},{8,11},{9,12},{10,... | collective-permute-start | bytes 393224 | tf_op jit(solution)/shard_map/ppermute | solution.py:86
  108.8 1.3 copy-start.3
  138.7 1.8 copy-start.8
  140.4 3.2 %copy-start.5 = (bf16[1,512,4096]{2,1,0:T(8,128)(2,1)S(1)}, bf16[1,512,4096]{2,1,0:T(8,128)(2,1)}, u32[]{:S(2)}) copy-start(bf16[1,512,4096]{2,1,0:T(8,128)(2,1)} %param.6) | copy-start | bytes 12582916
  142.3 1.3 copy-start.1
  143.6 1.3 copy-start.7
  145.6 14.8 %collective-permute-start.7 = (f32[256,256]{1,0:T(8,128)S(1)}, f32[256,256]{1,0:T(8,128)S(1)}, u32[]{:S(2)}, u32[]{:S(2)}) collective-permute-start(f32[256,256]{1,0:T(8,128)S(1)} %fusion.25), channel_id=1, source_target_pairs={{0,8},{8,0},{16,24},{24,16},{32,40},{40,32},{48,56},{56,48},{64,72... | collective-permute-start | bytes 786440 | tf_op jit(solution)/shard_map/ppermute | solution.py:80
  147.3 31.4 %collective-permute-start.5 = (bf16[512,128]{1,0:T(8,128)(2,1)S(1)}, bf16[512,128]{1,0:T(8,128)(2,1)S(1)}, u32[]{:S(2)}, u32[]{:S(2)}) collective-permute-start(bf16[512,128]{1,0:T(8,128)(2,1)S(1)} %get-tuple-element.15), channel_id=1, source_target_pairs={{0,2},{1,3},{2,4},{3,5},{4,6},{5,7},{6,0},{7,1},{8,10},{9,11},{10,... | collective-permute-start | bytes 393224 | tf_op jit(solution)/shard_map/ppermute | solution.py:86
  160.3 32.3 %collective-permute-start.6 = (bf16[512,128]{1,0:T(8,128)(2,1)S(1)}, bf16[512,128]{1,0:T(8,128)(2,1)S(1)}, u32[]{:S(2)}, u32[]{:S(2)}) collective-permute-start(bf16[512,128]{1,0:T(8,128)(2,1)S(1)} %get-tuple-element.14), channel_id=1, source_target_pairs={{0,1},{1,2},{2,3},{3,4},{4,5},{5,6},{6,7},{7,0},{8,9},{9,10},{10,1... | collective-permute-start | bytes 393224 | tf_op jit(solution)/shard_map/ppermute | solution.py:86
  163.1 9.0 %collective-permute-start.8 = (f32[256,256]{1,0:T(8,128)S(1)}, f32[256,256]{1,0:T(8,128)S(1)}, u32[]{:S(2)}, u32[]{:S(2)}) collective-permute-start(f32[256,256]{1,0:T(8,128)S(1)} %add.24), channel_id=1, source_target_pairs={{0,128},{8,136},{16,144},{24,152},{32,160},{40,168},{48,176},{56,1... | collective-permute-start | bytes 786440 | tf_op jit(solution)/shard_map/ppermute | solution.py:80
  172.9 15.6 %all-to-all-start.4 = ((f32[8,32,256]{2,1,0:T(8,128)}), f32[8,32,256]{2,1,0:T(8,128)S(1)}, u32[]{:S(2)}, u32[]{:S(2)}) async-start(f32[8,32,256]{2,1,0:T(8,128)} %bitcast.27), calls=%async_computation.4 | async-start | bytes 524288 | tf_op jit(solution)/shard_map/all_to_all | solution.py:109
  189.2 13.8 %all-to-all-start.5 = ((f32[8,32,256]{2,1,0:T(8,128)}), f32[8,32,256]{2,1,0:T(8,128)S(1)}, u32[]{:S(2)}, u32[]{:S(2)}) async-start(f32[8,32,256]{2,1,0:T(8,128)} %broadcast_in_dim.8), calls=%async_computation.5 | async-start | bytes 524288 | tf_op jit(solution)/shard_map/all_to_all | solution.py:20
  192.6 2.3 copy-start.2
  242.0 10.9 %collective-permute-start.9 = (bf16[512,128]{1,0:T(8,128)(2,1)S(1)}, bf16[512,128]{1,0:T(8,128)(2,1)S(1)}, u32[]{:S(2)}, u32[]{:S(2)}) collective-permute-start(bf16[512,128]{1,0:T(8,128)(2,1)S(1)} %get-tuple-element.12), channel_id=1, source_target_pairs={{0,7},{1,0},{2,1},{3,2},{4,3},{5,4},{6,5},{7,6},{8,15},{9,8},{10,9... | collective-permute-start | bytes 393224 | tf_op jit(solution)/shard_map/ppermute | solution.py:86
  245.0 11.1 %collective-permute-start.10 = (bf16[512,128]{1,0:T(8,128)(2,1)S(1)}, bf16[512,128]{1,0:T(8,128)(2,1)S(1)}, u32[]{:S(2)}, u32[]{:S(2)}) collective-permute-start(bf16[512,128]{1,0:T(8,128)(2,1)S(1)} %get-tuple-element.11), channel_id=1, source_target_pairs={{0,6},{1,7},{2,0},{3,1},{4,2},{5,3},{6,4},{7,5},{8,14},{9,15},{10,... | collective-permute-start | bytes 393224 | tf_op jit(solution)/shard_map/ppermute | solution.py:86
  246.6 9.5 %collective-permute-start.11 = (bf16[512,128]{1,0:T(8,128)(2,1)S(1)}, bf16[512,128]{1,0:T(8,128)(2,1)S(1)}, u32[]{:S(2)}, u32[]{:S(2)}) collective-permute-start(bf16[512,128]{1,0:T(8,128)(2,1)S(1)} %get-tuple-element.10), channel_id=1, source_target_pairs={{0,5},{1,6},{2,7},{3,0},{4,1},{5,2},{6,3},{7,4},{8,13},{9,14},{10,... | collective-permute-start | bytes 393224 | tf_op jit(solution)/shard_map/ppermute | solution.py:86
  248.0 8.2 %collective-permute-start.12 = (bf16[512,128]{1,0:T(8,128)(2,1)S(1)}, bf16[512,128]{1,0:T(8,128)(2,1)S(1)}, u32[]{:S(2)}, u32[]{:S(2)}) collective-permute-start(bf16[512,128]{1,0:T(8,128)(2,1)S(1)} %get-tuple-element.9), channel_id=1, source_target_pairs={{0,4},{1,5},{2,6},{3,7},{4,0},{5,1},{6,2},{7,3},{8,12},{9,13},{10,... | collective-permute-start | bytes 393224 | tf_op jit(solution)/shard_map/ppermute | solution.py:86
  249.2 8.9 %collective-permute-start.13 = (bf16[512,128]{1,0:T(8,128)(2,1)S(1)}, bf16[512,128]{1,0:T(8,128)(2,1)S(1)}, u32[]{:S(2)}, u32[]{:S(2)}) collective-permute-start(bf16[512,128]{1,0:T(8,128)(2,1)S(1)} %get-tuple-element.8), channel_id=1, source_target_pairs={{0,3},{1,4},{2,5},{3,6},{4,7},{5,0},{6,1},{7,2},{8,11},{9,12},{10,... | collective-permute-start | bytes 393224 | tf_op jit(solution)/shard_map/ppermute | solution.py:86
  252.9 6.4 %collective-permute-start.14 = (bf16[512,128]{1,0:T(8,128)(2,1)S(1)}, bf16[512,128]{1,0:T(8,128)(2,1)S(1)}, u32[]{:S(2)}, u32[]{:S(2)}) collective-permute-start(bf16[512,128]{1,0:T(8,128)(2,1)S(1)} %get-tuple-element.7), channel_id=1, source_target_pairs={{0,2},{1,3},{2,4},{3,5},{4,6},{5,7},{6,0},{7,1},{8,10},{9,11},{10,... | collective-permute-start | bytes 393224 | tf_op jit(solution)/shard_map/ppermute | solution.py:86
  256.1 7.4 %collective-permute-start.15 = (bf16[512,128]{1,0:T(8,128)(2,1)S(1)}, bf16[512,128]{1,0:T(8,128)(2,1)S(1)}, u32[]{:S(2)}, u32[]{:S(2)}) collective-permute-start(bf16[512,128]{1,0:T(8,128)(2,1)S(1)} %get-tuple-element.6), channel_id=1, source_target_pairs={{0,1},{1,2},{2,3},{3,4},{4,5},{5,6},{6,7},{7,0},{8,9},{9,10},{10,1... | collective-permute-start | bytes 393224 | tf_op jit(solution)/shard_map/ppermute | solution.py:86
where the time goes:
time: 270 us; the launch traced here: 265 us
  Pallas kernels  53.7 us (20%)
  blocking collectives  50.1 us (19%)
  starting transfers between devices  49.6 us (18%)
  waiting for transfers between devices  45.5 us (17%)
  local copies, waits for them, and re-layouts  29 us (11%)
  matrix products  23.9 us (9%)
  other arithmetic  12.7 us (5%)
    pallas_call x2, Pallas kernels, inverse_factor(): pl.pallas_call(functools.partial(_factor_kernel, panel_rows=64), out_shap...  53.7 us
    ppermute x14, starting transfers between devices, shifted(): return lax.ppermute(x, axis, [(j, (j + s) % n) for j in range(n)])  36.8 us
    all_to_all x1, blocking collectives, sum_by_axis(): lax.all_to_all(nearer, far, split_axis=0, concat_axis=0, tiled=True)  36.3 us
    all_to_all x2, waiting for transfers between devices, copy_for_each(): lax.all_to_all(jnp.broadcast_to(x[None], (devices, *x.shape)), axis, 0, 0...  21.3 us
    unnamed x30, local copies, waits for them, and re-layouts  11.3 us
    ppermute x14, waiting for transfers between devices, shifted(): return lax.ppermute(x, axis, [(j, (j + s) % n) for j in range(n)])  9.42 us
    another operation x2, local copies, waits for them, and re-layouts, in_blocks(): x.reshape(*lengths[:dim], devices, lengths[dim] // devices, *lengths[dim...  9.16 us
    all_to_all x1, waiting for transfers between devices, ring_sum(): own = lax.all_to_all(parts, axis, 0, 0, tiled=True).sum(axis=0)  9.05 us
  transfers between devices with their start and end apart: 19, of which 8 were waited for; matrix products, arithmetic and copies ran while one was open for 9% of the time, Pallas kernels for 10%

commit v1 on v0

--- a/solution.py
+++ b/solution.py
@@ -127,7 +127,6 @@
     r_ref[:, :n] = a_ref[...]
     r_ref[:, n:] = jnp.where(rows_i == cols_i, 1.0, 0.0).astype(jnp.float32)
     sub = lax.broadcasted_iota(jnp.int32, (panel_rows, 1), 0)
-    lane = lax.broadcasted_iota(jnp.int32, (panel_rows, 128), 1)
     lane_wide = lax.broadcasted_iota(jnp.int32, (1, 2 * n), 1)
     for p in range(n // panel_rows):
         r0 = panel_rows * p
@@ -135,7 +134,7 @@
         for r in range(panel_rows):
             j = r0 + r
             part = panel[:, (j // 128) * 128:(j // 128 + 1) * 128]
-            column = jnp.sum(jnp.where(lane == (j % 128), part, 0.0), axis=1, keepdims=True)
+            column = part[:, j % 128:j % 128 + 1]
             inv = lax.rsqrt(column[r:r + 1, :])
             row = jnp.where(lane_wide < j, 0.0, panel[r:r + 1, :] * inv)
             mult = jnp.where(sub > r, column * inv, 0.0)

time: 270 us -> 267 us (0.989)
  matrix products: 23.9 us -> 35.2 us
  starting transfers between devices: 49.6 us -> 39.6 us
  Pallas kernels: 53.7 us -> 50.1 us
    dot_general x1, matrix products: 1.3 us -> 12.6 us  [shards(): jnp.dot(features, basis, preferred_element_type=jnp.float32)]
    ppermute x14, starting transfers between devices: 36.8 us -> 26.8 us  [shifted(): return lax.ppermute(x, axis, [(j, (j + s) % n) for j in range(n)])]
    pallas_call x2, Pallas kernels: 53.7 us -> 50.1 us  [inverse_factor(): pl.pallas_call(functools.partial(_factor_kernel, panel_rows=64), out_shap...]
  transfers between devices with their start and end apart: 19 -> 19, of which waited for: 8 -> 8; matrix products, arithmetic and copies ran while one was open for 9% -> 13% of each run, Pallas kernels for 10% -> 10%
where the time goes in v1:
time: 267 us; the launch traced here: 263 us
  Pallas kernels  50.1 us (19%)
  blocking collectives  49.9 us (19%)
  waiting for transfers between devices  45.6 us (17%)
  starting transfers between devices  39.6 us (15%)
  matrix products  35.2 us (13%)
  local copies, waits for them, and re-layouts  29 us (11%)
  other arithmetic  12.9 us (5%)
    pallas_call x2, Pallas kernels, inverse_factor(): pl.pallas_call(functools.partial(_factor_kernel, panel_rows=64), out_shap...  50.1 us
    all_to_all x1, blocking collectives, sum_by_axis(): lax.all_to_all(nearer, far, split_axis=0, concat_axis=0, tiled=True)  36.3 us
    ppermute x14, starting transfers between devices, shifted(): return lax.ppermute(x, axis, [(j, (j + s) % n) for j in range(n)])  26.8 us
    all_to_all x2, waiting for transfers between devices, copy_for_each(): lax.all_to_all(jnp.broadcast_to(x[None], (devices, *x.shape)), axis, 0, 0...  21.3 us
    dot_general x1, matrix products, shards(): jnp.dot(features, basis, preferred_element_type=jnp.float32)  12.6 us
    unnamed x30, local copies, waits for them, and re-layouts  11.3 us
    ppermute x14, waiting for transfers between devices, shifted(): return lax.ppermute(x, axis, [(j, (j + s) % n) for j in range(n)])  9.5 us
    another operation x2, local copies, waits for them, and re-layouts, in_blocks(): x.reshape(*lengths[:dim], devices, lengths[dim] // devices, *lengths[dim...  9.16 us
  transfers between devices with their start and end apart: 19, of which 8 were waited for; matrix products, arithmetic and copies ran while one was open for 13% of the time, Pallas kernels for 10%

profile of v1, /device:TPU:8, one launch (start us, length us, event | category | flops | bytes accessed | tf_op | source)
XLA Modules:
  0.0 262.8 jit_solution(6968541557900634577)
XLA Ops:
  0.0 6.0 %fusion.13 = bf16[512,512]{1,0:T(8,128)(2,1)S(1)} fusion(bf16[1,512,4096]{2,1,0:T(8,128)(2,1)} %param.7), kind=kOutput, calls=%fused_computation.25 | convolution fusion | flops 2147745792 | bytes 4718592 | tf_op jit(solution)/shard_map/dot_general | solution.py:174
  6.0 1.3 fusion.16
  7.3 5.9 %fusion = f32[4096,256]{0,1:T(8,128)} fusion(bf16[1,512,4096]{2,1,0:T(8,128)(2,1)} %param.6, bf16[512,512]{1,0:T(8,128)(2,1)S(1)} %fusion.13, bf16[512,256]{1,0:T(8,128)(2,1)S(1)} %fusion.16), kind=kOutput, calls=%fused_computation.1 | convolution fusion | flops 1209139200 | bytes 9175040 | tf_op jit(solution)/shard_map/dot_general | solution.py:181
  13.2 6.6 %reshape_reshape.6 = f32[16,2,128,256]{2,1,0,3:T(2,128)} reshape(f32[4096,256]{0,1:T(8,128)} %fusion) | data formatting | bytes 8388608 | tf_op jit(solution)/shard_map/reshape;reshape | solution.py:38
  19.8 2.5 copy.44
  22.3 8.2 %all_to_all.30 = f32[2,16,128,256]{2,1,3,0:T(8,128)} all-to-all(f32[2,16,128,256]{2,1,3,0:T(8,128)S(1)} %bitcast.129), channel_id=1, replica_groups=mesh['dp_0'=2,'dp_1'=8,'dp_2'=2,'blk'=8] {'dp_2'}, dimensions={0} | all-to-all | bytes 8388608 | tf_op jit(solution)/shard_map/all_to_all | solution.py:44
  30.5 2.6 reduce_sum.30
  33.4 36.3 %all_to_all.31 = bf16[16,128,256]{1,2,0:T(8,128)(2,1)S(1)} all-to-all(bf16[16,128,256]{1,2,0:T(8,128)(2,1)S(1)} %copy.21), channel_id=1, replica_groups=mesh['dp_0'=2,'dp_1'=8,'dp_2'=2,'blk'=8] {'dp_0','dp_1'}, dimensions={0} | all-to-all | bytes 2097152 | tf_op jit(solution)/shard_map/all_to_all | solution.py:52
  71.0 4.8 %all-to-all-start.2 = ((bf16[16,128,256]{2,1,0:T(8,128)(2,1)}), bf16[16,128,256]{2,1,0:T(8,128)(2,1)S(1)}, u32[]{:S(2)}, u32[]{:S(2)}) async-start(bf16[16,128,256]{2,1,0:T(8,128)(2,1)} %broadcast_in_dim.6), calls=%async_computation.2 | async-start | bytes 2097152 | tf_op jit(solution)/shard_map/all_to_all | solution.py:20
  75.8 1.6 fusion.34
  78.3 2.6 collective-permute-start
  80.9 3.1 %collective-permute-start.1 = (bf16[512,128]{1,0:T(8,128)(2,1)}, bf16[512,128]{1,0:T(8,128)(2,1)}, u32[]{:S(2)}, u32[]{:S(2)}) collective-permute-start(bf16[512,128]{1,0:T(8,128)(2,1)} %get-tuple-element.19), channel_id=1, source_target_pairs={{0,6},{1,7},{2,0},{3,1},{4,2},{5,3},{6,4},{7,5},{8,14},{9,15},{10,... | collective-permute-start | bytes 393224 | tf_op jit(solution)/shard_map/ppermute | solution.py:86
  85.3 3.7 %collective-permute-start.4 = (bf16[512,128]{1,0:T(8,128)(2,1)S(1)}, bf16[512,128]{1,0:T(8,128)(2,1)}, u32[]{:S(2)}, u32[]{:S(2)}) collective-permute-start(bf16[512,128]{1,0:T(8,128)(2,1)S(1)} %get-tuple-element.16), channel_id=1, source_target_pairs={{0,3},{1,4},{2,5},{3,6},{4,7},{5,0},{6,1},{7,2},{8,11},{9,12},{10,... | collective-permute-start | bytes 393224 | tf_op jit(solution)/shard_map/ppermute | solution.py:86
  89.0 14.0 %all-to-all-done.2 = bf16[16,128,256]{2,1,0:T(8,128)(2,1)S(1)} async-done(((bf16[16,128,256]{2,1,0:T(8,128)(2,1)}), bf16[16,128,256]{2,1,0:T(8,128)(2,1)S(1)}, u32[]{:S(2)}, u32[]{:S(2)}) %all-to-all-start.2) | async-done | bytes 1048608 | tf_op jit(solution)/shard_map/all_to_all | solution.py:20
  103.2 5.4 %all_to_all.32 = bf16[2,16,128,256]{3,2,1,0:T(8,128)(2,1)S(1)} all-to-all(bf16[2,16,128,256]{3,2,1,0:T(8,128)(2,1)S(1)} %broadcast_in_dim.7), channel_id=1, replica_groups=mesh['dp_0'=2,'dp_1'=8,'dp_2'=2,'blk'=8] {'dp_2'}, dimensions={0} | all-to-all | bytes 4194304 | tf_op jit(solution)/shard_map/all_to_all | solution.py:20
  108.6 1.3 copy-done.3
  111.6 25.0 %shard_map.46 = f32[256,256]{1,0:T(8,128)} custom-call(f32[256,256]{1,0:T(8,128)} %fusion.36.a_ref), custom_call_target="tpu_custom_call" | custom-call | tf_op jit(solution)/shard_map/pallas_call | solution.py:156
  136.6 1.8 copy.24
  138.4 1.8 convolution_convert_fusion
  140.3 1.3 copy-done.1
  141.6 12.6 %fusion.21 = bf16[256,512]{1,0:T(8,128)(2,1)S(1)} fusion(bf16[4096,256]{1,0:T(8,128)(2,1)S(1)} %convolution_convert_fusion, bf16[1,512,4096]{2,1,0:T(8,128)(2,1)S(1)} %copy-done.5), kind=kOutput, calls=%fused_computation.27 | convolution fusion | flops 1073872896 | bytes 6553600 | tf_op jit(solution)/shard_map/dot_general | solution.py:188
  155.1 1.6 bitcast_dynamic-update-slice_fusion.13
  156.6 1.6 collective-permute-start.5
  158.2 1.6 bitcast_dynamic-update-slice_fusion.12
  159.8 2.7 %collective-permute-start.6 = (bf16[512,128]{1,0:T(8,128)(2,1)S(1)}, bf16[512,128]{1,0:T(8,128)(2,1)S(1)}, u32[]{:S(2)}, u32[]{:S(2)}) collective-permute-start(bf16[512,128]{1,0:T(8,128)(2,1)S(1)} %get-tuple-element.14), channel_id=1, source_target_pairs={{0,1},{1,2},{2,3},{3,4},{4,5},{5,6},{6,7},{7,0},{8,9},{9,10},{10,1... | collective-permute-start | bytes 393224 | tf_op jit(solution)/shard_map/ppermute | solution.py:86
  162.7 1.6 bitcast_dynamic-update-slice_fusion.11
  164.2 1.6 bitcast_dynamic-update-slice_fusion.10
  165.8 5.8 %collective-permute-done.8 = f32[256,256]{1,0:T(8,128)S(1)} collective-permute-done((f32[256,256]{1,0:T(8,128)S(1)}, f32[256,256]{1,0:T(8,128)S(1)}, u32[]{:S(2)}, u32[]{:S(2)}) %collective-permute-start.8) | collective-permute-done | bytes 262176 | tf_op jit(solution)/shard_map/ppermute | solution.py:80
  172.3 4.3 %all-to-all-start.4 = ((f32[8,32,256]{2,1,0:T(8,128)}), f32[8,32,256]{2,1,0:T(8,128)S(1)}, u32[]{:S(2)}, u32[]{:S(2)}) async-start(f32[8,32,256]{2,1,0:T(8,128)} %bitcast.27), calls=%async_computation.4 | async-start | bytes 524288 | tf_op jit(solution)/shard_map/all_to_all | solution.py:109
  176.6 1.6 bitcast_dynamic-update-slice_fusion.9
  178.8 9.1 %all-to-all-done.4 = f32[8,32,256]{2,1,0:T(8,128)S(1)} async-done(((f32[8,32,256]{2,1,0:T(8,128)}), f32[8,32,256]{2,1,0:T(8,128)S(1)}, u32[]{:S(2)}, u32[]{:S(2)}) %all-to-all-start.4) | async-done | bytes 262176 | tf_op jit(solution)/shard_map/all_to_all | solution.py:109
  188.6 3.4 %all-to-all-start.5 = ((f32[8,32,256]{2,1,0:T(8,128)}), f32[8,32,256]{2,1,0:T(8,128)S(1)}, u32[]{:S(2)}, u32[]{:S(2)}) async-start(f32[8,32,256]{2,1,0:T(8,128)} %broadcast_in_dim.8), calls=%async_computation.5 | async-start | bytes 524288 | tf_op jit(solution)/shard_map/all_to_all | solution.py:20
  192.8 1.6 fusion.33
  195.1 7.3 %all-to-all-done.5 = f32[8,32,256]{2,1,0:T(8,128)S(1)} async-done(((f32[8,32,256]{2,1,0:T(8,128)}), f32[8,32,256]{2,1,0:T(8,128)S(1)}, u32[]{:S(2)}, u32[]{:S(2)}) %all-to-all-start.5) | async-done | bytes 262176 | tf_op jit(solution)/shard_map/all_to_all | solution.py:20
  203.3 1.7 convert_add_fusion
  205.0 1.8 copy.28
  206.8 1.8 fusion.35.a_ref
  208.5 25.0 %shard_map.47 = f32[256,256]{1,0:T(8,128)} custom-call(f32[256,256]{1,0:T(8,128)} %fusion.35.a_ref), custom_call_target="tpu_custom_call" | custom-call | tf_op jit(solution)/shard_map/pallas_call | solution.py:156
  233.6 1.3 fusion.38
  234.9 1.5 fusion.39
  236.8 2.3 fusion.1
  239.8 3.0 %collective-permute-start.9 = (bf16[512,128]{1,0:T(8,128)(2,1)S(1)}, bf16[512,128]{1,0:T(8,128)(2,1)S(1)}, u32[]{:S(2)}, u32[]{:S(2)}) collective-permute-start(bf16[512,128]{1,0:T(8,128)(2,1)S(1)} %get-tuple-element.12), channel_id=1, source_target_pairs={{0,7},{1,0},{2,1},{3,2},{4,3},{5,4},{6,5},{7,6},{8,15},{9,8},{10,9... | collective-permute-start | bytes 393224 | tf_op jit(solution)/shard_map/ppermute | solution.py:86
  242.8 1.7 collective-permute-start.10
  246.9 3.7 %collective-permute-start.13 = (bf16[512,128]{1,0:T(8,128)(2,1)S(1)}, bf16[512,128]{1,0:T(8,128)(2,1)S(1)}, u32[]{:S(2)}, u32[]{:S(2)}) collective-permute-start(bf16[512,128]{1,0:T(8,128)(2,1)S(1)} %get-tuple-element.8), channel_id=1, source_target_pairs={{0,3},{1,4},{2,5},{3,6},{4,7},{5,0},{6,1},{7,2},{8,11},{9,12},{10,... | collective-permute-start | bytes 393224 | tf_op jit(solution)/shard_map/ppermute | solution.py:86
  251.6 2.2 collective-permute-done.10
  253.9 1.8 collective-permute-done.13
  257.0 4.2 %collective-permute-done.15 = bf16[512,128]{1,0:T(8,128)(2,1)S(1)} collective-permute-done((bf16[512,128]{1,0:T(8,128)(2,1)S(1)}, bf16[512,128]{1,0:T(8,128)(2,1)S(1)}, u32[]{:S(2)}, u32[]{:S(2)}) %collective-permute-start.15) | collective-permute-done | bytes 131104 | tf_op jit(solution)/shard_map/ppermute | solution.py:86
  261.2 1.4 fusion.31
  (64 shorter events, 16.8 us)
Async XLA Ops:
  0.0 6.0 %copy-start = (bf16[1,4096,256]{2,1,0:T(8,128)(2,1)S(1)}, bf16[1,4096,256]{2,1,0:T(8,128)(2,1)}, u32[]{:S(2)}) copy-start(bf16[1,4096,256]{2,1,0:T(8,128)(2,1)} %param.8) | copy-start | bytes 6291460
  0.0 6.0 %copy-start.4 = (bf16[1,512,4096]{2,1,0:T(8,128)(2,1)S(1)}, bf16[1,512,4096]{2,1,0:T(8,128)(2,1)}, u32[]{:S(2)}) copy-start(bf16[1,512,4096]{2,1,0:T(8,128)(2,1)} %param.6) | copy-start | bytes 12582916
  6.0 1.3 copy-start.6
  71.0 31.9 %all-to-all-start.2 = ((bf16[16,128,256]{2,1,0:T(8,128)(2,1)}), bf16[16,128,256]{2,1,0:T(8,128)(2,1)S(1)}, u32[]{:S(2)}, u32[]{:S(2)}) async-start(bf16[16,128,256]{2,1,0:T(8,128)(2,1)} %broadcast_in_dim.6), calls=%async_computation.2 | async-start | bytes 2097152 | tf_op jit(solution)/shard_map/all_to_all | solution.py:20
  78.3 76.5 %collective-permute-start = (bf16[512,128]{1,0:T(8,128)(2,1)}, bf16[512,128]{1,0:T(8,128)(2,1)}, u32[]{:S(2)}, u32[]{:S(2)}) collective-permute-start(bf16[512,128]{1,0:T(8,128)(2,1)} %get-tuple-element.20), channel_id=1, source_target_pairs={{0,7},{1,0},{2,1},{3,2},{4,3},{5,4},{6,5},{7,6},{8,15},{9,8},{10,9... | collective-permute-start | bytes 393224 | tf_op jit(solution)/shard_map/ppermute | solution.py:86
  80.9 75.7 %collective-permute-start.1 = (bf16[512,128]{1,0:T(8,128)(2,1)}, bf16[512,128]{1,0:T(8,128)(2,1)}, u32[]{:S(2)}, u32[]{:S(2)}) collective-permute-start(bf16[512,128]{1,0:T(8,128)(2,1)} %get-tuple-element.19), channel_id=1, source_target_pairs={{0,6},{1,7},{2,0},{3,1},{4,2},{5,3},{6,4},{7,5},{8,14},{9,15},{10,... | collective-permute-start | bytes 393224 | tf_op jit(solution)/shard_map/ppermute | solution.py:86
  84.0 78.6 %collective-permute-start.2 = (bf16[512,128]{1,0:T(8,128)(2,1)}, bf16[512,128]{1,0:T(8,128)(2,1)}, u32[]{:S(2)}, u32[]{:S(2)}) collective-permute-start(bf16[512,128]{1,0:T(8,128)(2,1)} %get-tuple-element.18), channel_id=1, source_target_pairs={{0,5},{1,6},{2,7},{3,0},{4,1},{5,2},{6,3},{7,4},{8,13},{9,14},{10,... | collective-permute-start | bytes 393224 | tf_op jit(solution)/shard_map/ppermute | solution.py:86
  84.3 79.9 %collective-permute-start.3 = (bf16[512,128]{1,0:T(8,128)(2,1)}, bf16[512,128]{1,0:T(8,128)(2,1)}, u32[]{:S(2)}, u32[]{:S(2)}) collective-permute-start(bf16[512,128]{1,0:T(8,128)(2,1)} %get-tuple-element.17), channel_id=1, source_target_pairs={{0,4},{1,5},{2,6},{3,7},{4,0},{5,1},{6,2},{7,3},{8,12},{9,13},{10,... | collective-permute-start | bytes 393224 | tf_op jit(solution)/shard_map/ppermute | solution.py:86
  85.3 91.3 %collective-permute-start.4 = (bf16[512,128]{1,0:T(8,128)(2,1)S(1)}, bf16[512,128]{1,0:T(8,128)(2,1)}, u32[]{:S(2)}, u32[]{:S(2)}) collective-permute-start(bf16[512,128]{1,0:T(8,128)(2,1)S(1)} %get-tuple-element.16), channel_id=1, source_target_pairs={{0,3},{1,4},{2,5},{3,6},{4,7},{5,0},{6,1},{7,2},{8,11},{9,12},{10,... | collective-permute-start | bytes 393224 | tf_op jit(solution)/shard_map/ppermute | solution.py:86
  108.6 1.3 copy-start.3
  136.6 1.8 copy-start.8
  138.4 3.2 %copy-start.5 = (bf16[1,512,4096]{2,1,0:T(8,128)(2,1)S(1)}, bf16[1,512,4096]{2,1,0:T(8,128)(2,1)}, u32[]{:S(2)}) copy-start(bf16[1,512,4096]{2,1,0:T(8,128)(2,1)} %param.6) | copy-start | bytes 12582916
  140.3 1.3 copy-start.1
  141.6 12.6 %copy-start.7 = (bf16[512,512]{1,0:T(8,128)(2,1)S(1)}, bf16[512,512]{1,0:T(8,128)(2,1)}, u32[]{:S(2)}) copy-start(bf16[512,512]{1,0:T(8,128)(2,1)} %copy-done.6) | copy-start | bytes 1572868
  154.8 4.9 %collective-permute-start.7 = (f32[256,256]{1,0:T(8,128)S(1)}, f32[256,256]{1,0:T(8,128)S(1)}, u32[]{:S(2)}, u32[]{:S(2)}) collective-permute-start(f32[256,256]{1,0:T(8,128)S(1)} %fusion.25), channel_id=1, source_target_pairs={{0,8},{8,0},{16,24},{24,16},{32,40},{40,32},{48,56},{56,48},{64,72... | collective-permute-start | bytes 786440 | tf_op jit(solution)/shard_map/ppermute | solution.py:80
  156.6 21.6 %collective-permute-start.5 = (bf16[512,128]{1,0:T(8,128)(2,1)S(1)}, bf16[512,128]{1,0:T(8,128)(2,1)S(1)}, u32[]{:S(2)}, u32[]{:S(2)}) collective-permute-start(bf16[512,128]{1,0:T(8,128)(2,1)S(1)} %get-tuple-element.15), channel_id=1, source_target_pairs={{0,2},{1,3},{2,4},{3,5},{4,6},{5,7},{6,0},{7,1},{8,10},{9,11},{10,... | collective-permute-start | bytes 393224 | tf_op jit(solution)/shard_map/ppermute | solution.py:86
  159.8 32.3 %collective-permute-start.6 = (bf16[512,128]{1,0:T(8,128)(2,1)S(1)}, bf16[512,128]{1,0:T(8,128)(2,1)S(1)}, u32[]{:S(2)}, u32[]{:S(2)}) collective-permute-start(bf16[512,128]{1,0:T(8,128)(2,1)S(1)} %get-tuple-element.14), channel_id=1, source_target_pairs={{0,1},{1,2},{2,3},{3,4},{4,5},{5,6},{6,7},{7,0},{8,9},{9,10},{10,1... | collective-permute-start | bytes 393224 | tf_op jit(solution)/shard_map/ppermute | solution.py:86
  162.6 9.0 %collective-permute-start.8 = (f32[256,256]{1,0:T(8,128)S(1)}, f32[256,256]{1,0:T(8,128)S(1)}, u32[]{:S(2)}, u32[]{:S(2)}) collective-permute-start(f32[256,256]{1,0:T(8,128)S(1)} %add.24), channel_id=1, source_target_pairs={{0,128},{8,136},{16,144},{24,152},{32,160},{40,168},{48,176},{56,1... | collective-permute-start | bytes 786440 | tf_op jit(solution)/shard_map/ppermute | solution.py:80
  172.3 15.6 %all-to-all-start.4 = ((f32[8,32,256]{2,1,0:T(8,128)}), f32[8,32,256]{2,1,0:T(8,128)S(1)}, u32[]{:S(2)}, u32[]{:S(2)}) async-start(f32[8,32,256]{2,1,0:T(8,128)} %bitcast.27), calls=%async_computation.4 | async-start | bytes 524288 | tf_op jit(solution)/shard_map/all_to_all | solution.py:109
  188.6 13.8 %all-to-all-start.5 = ((f32[8,32,256]{2,1,0:T(8,128)}), f32[8,32,256]{2,1,0:T(8,128)S(1)}, u32[]{:S(2)}, u32[]{:S(2)}) async-start(f32[8,32,256]{2,1,0:T(8,128)} %broadcast_in_dim.8), calls=%async_computation.5 | async-start | bytes 524288 | tf_op jit(solution)/shard_map/all_to_all | solution.py:20
  192.1 2.3 copy-start.2
  239.8 10.8 %collective-permute-start.9 = (bf16[512,128]{1,0:T(8,128)(2,1)S(1)}, bf16[512,128]{1,0:T(8,128)(2,1)S(1)}, u32[]{:S(2)}, u32[]{:S(2)}) collective-permute-start(bf16[512,128]{1,0:T(8,128)(2,1)S(1)} %get-tuple-element.12), channel_id=1, source_target_pairs={{0,7},{1,0},{2,1},{3,2},{4,3},{5,4},{6,5},{7,6},{8,15},{9,8},{10,9... | collective-permute-start | bytes 393224 | tf_op jit(solution)/shard_map/ppermute | solution.py:86
  242.8 11.0 %collective-permute-start.10 = (bf16[512,128]{1,0:T(8,128)(2,1)S(1)}, bf16[512,128]{1,0:T(8,128)(2,1)S(1)}, u32[]{:S(2)}, u32[]{:S(2)}) collective-permute-start(bf16[512,128]{1,0:T(8,128)(2,1)S(1)} %get-tuple-element.11), channel_id=1, source_target_pairs={{0,6},{1,7},{2,0},{3,1},{4,2},{5,3},{6,4},{7,5},{8,14},{9,15},{10,... | collective-permute-start | bytes 393224 | tf_op jit(solution)/shard_map/ppermute | solution.py:86
  244.5 9.4 %collective-permute-start.11 = (bf16[512,128]{1,0:T(8,128)(2,1)S(1)}, bf16[512,128]{1,0:T(8,128)(2,1)S(1)}, u32[]{:S(2)}, u32[]{:S(2)}) collective-permute-start(bf16[512,128]{1,0:T(8,128)(2,1)S(1)} %get-tuple-element.10), channel_id=1, source_target_pairs={{0,5},{1,6},{2,7},{3,0},{4,1},{5,2},{6,3},{7,4},{8,13},{9,14},{10,... | collective-permute-start | bytes 393224 | tf_op jit(solution)/shard_map/ppermute | solution.py:86
  245.6 8.3 %collective-permute-start.12 = (bf16[512,128]{1,0:T(8,128)(2,1)S(1)}, bf16[512,128]{1,0:T(8,128)(2,1)S(1)}, u32[]{:S(2)}, u32[]{:S(2)}) collective-permute-start(bf16[512,128]{1,0:T(8,128)(2,1)S(1)} %get-tuple-element.9), channel_id=1, source_target_pairs={{0,4},{1,5},{2,6},{3,7},{4,0},{5,1},{6,2},{7,3},{8,12},{9,13},{10,... | collective-permute-start | bytes 393224 | tf_op jit(solution)/shard_map/ppermute | solution.py:86
  246.9 8.9 %collective-permute-start.13 = (bf16[512,128]{1,0:T(8,128)(2,1)S(1)}, bf16[512,128]{1,0:T(8,128)(2,1)S(1)}, u32[]{:S(2)}, u32[]{:S(2)}) collective-permute-start(bf16[512,128]{1,0:T(8,128)(2,1)S(1)} %get-tuple-element.8), channel_id=1, source_target_pairs={{0,3},{1,4},{2,5},{3,6},{4,7},{5,0},{6,1},{7,2},{8,11},{9,12},{10,... | collective-permute-start | bytes 393224 | tf_op jit(solution)/shard_map/ppermute | solution.py:86
  250.6 6.4 %collective-permute-start.14 = (bf16[512,128]{1,0:T(8,128)(2,1)S(1)}, bf16[512,128]{1,0:T(8,128)(2,1)S(1)}, u32[]{:S(2)}, u32[]{:S(2)}) collective-permute-start(bf16[512,128]{1,0:T(8,128)(2,1)S(1)} %get-tuple-element.7), channel_id=1, source_target_pairs={{0,2},{1,3},{2,4},{3,5},{4,6},{5,7},{6,0},{7,1},{8,10},{9,11},{10,... | collective-permute-start | bytes 393224 | tf_op jit(solution)/shard_map/ppermute | solution.py:86
  253.8 7.4 %collective-permute-start.15 = (bf16[512,128]{1,0:T(8,128)(2,1)S(1)}, bf16[512,128]{1,0:T(8,128)(2,1)S(1)}, u32[]{:S(2)}, u32[]{:S(2)}) collective-permute-start(bf16[512,128]{1,0:T(8,128)(2,1)S(1)} %get-tuple-element.6), channel_id=1, source_target_pairs={{0,1},{1,2},{2,3},{3,4},{4,5},{5,6},{6,7},{7,0},{8,9},{9,10},{10,1... | collective-permute-start | bytes 393224 | tf_op jit(solution)/shard_map/ppermute | solution.py:86
